TPU v7x, 32 devices: a whole 2x2x4 slice. The times are simulated.
32 devices in a mesh: fsdp: 8 (over z, y), dp: 4 (over x, core).
Axes of the slice: x: 2, y: 2, z: 4, core: 2. Of those that a mesh axis runs over, the one named last changes fastest.
Arguments:
- tokens: bfloat16 [32768, 768], P(('fsdp', 'dp')), may hold values from -6 to 6
- image_table: int32 [160, 3], P(('fsdp', 'dp')), may hold values from 0 to 996, as said below
- ln1_gain: bfloat16 [768], P('fsdp'), may hold values from 0.5 to 1.5
- ln1_bias: bfloat16 [768], P('fsdp'), may hold values from -3 to 3
- qkv_weight: bfloat16 [768, 2304], P('fsdp'), may hold values from -0.21875 to 0.21875
- qkv_bias: bfloat16 [2304], P('fsdp'), may hold values from -2 to 2
- out_weight: bfloat16 [768, 768], P('fsdp'), may hold values from -0.875 to 0.875
- out_bias: bfloat16 [768], P('fsdp'), may hold values from -2 to 2
- ln2_gain: bfloat16 [768], P('fsdp'), may hold values from 0.5 to 1.5
- ln2_bias: bfloat16 [768], P('fsdp'), may hold values from -3 to 3
- fc1_weight: bfloat16 [768, 3072], P('fsdp'), may hold values from -0.21875 to 0.21875
- fc1_bias: bfloat16 [3072], P('fsdp'), may hold values from -3 to 3
- fc2_weight: bfloat16 [3072, 768], P('fsdp'), may hold values from -0.109375 to 0.109375
- fc2_bias: bfloat16 [768], P('fsdp'), may hold values from -2 to 2
- frequencies: bfloat16 [768], P('fsdp'), may hold values from -0.796875 to 0.796875
- cotangent: bfloat16 [32768, 768], P(('fsdp', 'dp')), may hold values from -6 to 6
Outputs:
- block_out: bfloat16 [32768, 768], P(('fsdp', 'dp'))
- tokens_grad: bfloat16 [32768, 768], P(('fsdp', 'dp'))
- first_norm_gain_gradient: float32 [768], P('fsdp')
- ln1_bias_grad: float32 [768], P('fsdp')
- qkv_weight_grad: float32 [768, 2304], P('fsdp')
- qkv_bias_grad: float32 [2304], P('fsdp')
- out_weight_grad: float32 [768, 768], P('fsdp')
- out_bias_grad: float32 [768], P('fsdp')
- second_norm_gain_gradient: float32 [768], P('fsdp')
- ln2_bias_grad: float32 [768], P('fsdp')
- fc1_weight_grad: float32 [768, 3072], P('fsdp')
- fc1_bias_grad: float32 [3072], P('fsdp')
- fc2_weight_grad: float32 [3072, 768], P('fsdp')
- fc2_bias_grad: float32 [768], P('fsdp')
- frequencies_grad: float32 [768], P('fsdp')
- freq_grad_norm: float32 [], replicated
- other_grad_norm: float32 [], replicated
Inputs may be any that keep to these rules, and one draw needn't show every extreme that they name: `image_table`: rows 5b to 5b+4 describe bin b: either a 24x24 and a 20x20 image, or 24x24 and two 14x14, or two 20x20 and one 14x14, or one 20x20 and three 14x14, or five 14x14, laid end to end from offset 0 in the listed order; unused rows have height and width 0 and the offset where the used rows end. Grids are square.
All inputs are finite; a program needn't handle non-finite values.
Results may differ from a plain program's by a relative error of at most 0.015.
Values may be sent and summed in bfloat16 or wider, within the bound.
No kernel may reach another device: no remote copies, remote signals or barrier semaphores. Data moves between devices by JAX's collectives and lax.ppermute only.
A program may use at most 192 MiB of HBM per device.

v0:
```python
import jax
import jax.numpy as jnp
from jax import lax
from jax.sharding import PartitionSpec as P

H = 12
HD = 64
BIN = 1024
norm_eps = 1e-06
masked_score = -1e30
inv_sqrt_two_pi = 0.3989422804014327


def matmul(left, right):
    return jnp.dot(left, right, preferred_element_type=jnp.float32)


def matmul_left_t(left, right):
    return lax.dot_general(
        left, right, (((0,), (0,)), ((), ())), preferred_element_type=jnp.float32
    )


def matmul_right_t(left, right):
    return lax.dot_general(
        left, right, (((1,), (1,)), ((), ())), preferred_element_type=jnp.float32
    )


def image_layout(image_table, bin_count, bin_rows):
    slot_count = image_table.shape[0] // bin_count
    table = image_table.reshape(bin_count, slot_count, 3)
    offset = table[:, :, 0:1]
    height = table[:, :, 1:2]
    width = table[:, :, 2:3]
    place = jnp.arange(bin_rows, dtype=jnp.int32)[None, None, :]
    inside = ((place >= offset) & (place < offset + height * width)).astype(jnp.int32)
    live = jnp.sum(inside, axis=1)
    slot_ids = jnp.arange(slot_count, dtype=jnp.int32)[None, :, None]
    segment = jnp.sum(inside * slot_ids, axis=1) + slot_count * (1 - live)
    local_place = place[:, 0, :] - jnp.sum(inside * offset, axis=1)
    grid_width = jnp.maximum(jnp.sum(inside * width, axis=1), 1)
    grid_row = local_place // grid_width * live
    grid_col = local_place % grid_width * live
    return (
        segment,
        grid_row.reshape(-1).astype(jnp.float32),
        grid_col.reshape(-1).astype(jnp.float32),
    )


def rotary_tables(frequencies, grid_row, grid_col):
    half_width = frequencies.shape[0] // 2
    freq_float = frequencies.astype(jnp.float32)
    freq_row = freq_float[:half_width].reshape(H, HD // 2)
    freq_col = freq_float[half_width:].reshape(H, HD // 2)
    theta = grid_row[:, None, None] * freq_row[None] + grid_col[:, None, None] * freq_col[None]
    return (jnp.cos(theta), jnp.sin(theta))


def rotate(heads, cosine, sine):
    half_width = heads.shape[-1] // 2
    first = heads[..., :half_width]
    second = heads[..., half_width:]
    return jnp.concatenate(
        [first * cosine - second * sine, first * sine + second * cosine], axis=-1
    )


def layer_norm_forward(values):
    center = values - jnp.mean(values, axis=-1, keepdims=True)
    inverse_deviation = lax.rsqrt(jnp.mean(center * center, axis=-1, keepdims=True) + norm_eps)
    return (center * inverse_deviation, inverse_deviation)


def layer_norm_backward(
    gradient_norm_total, centered_normalized, inverse_deviation, norm_gain_vector
):
    gain_scaled_output = gradient_norm_total * norm_gain_vector
    return inverse_deviation * (
        gain_scaled_output
        - jnp.mean(gain_scaled_output, axis=-1, keepdims=True)
        - centered_normalized
        * jnp.mean(gain_scaled_output * centered_normalized, axis=-1, keepdims=True)
    )


def gelu_slope(values):
    return (
        0.5 * (1.0 + lax.erf(values * 0.7071067811865476))
        + values * jnp.exp(-0.5 * values * values) * inv_sqrt_two_pi
    )


def join_heads(stacked):
    return jnp.transpose(stacked, (1, 0, 2)).reshape(stacked.shape[1], H * HD)


def head_slice(matrix, head_index):
    return lax.dynamic_slice_in_dim(matrix, head_index * HD, HD, 1)


def attend_bin(packed):
    query, key_rows, value, segment = packed
    mask = segment[:, None] == segment[None, :]
    scale = HD ** (-0.5)

    def one_head(head_index):
        q_head = head_slice(query, head_index)
        k_head = head_slice(key_rows, head_index)
        v_head = head_slice(value, head_index)
        scores = jnp.where(mask, matmul_right_t(q_head, k_head) * scale, masked_score)
        top = jnp.max(scores, axis=-1, keepdims=True)
        log_total = top + jnp.log(jnp.sum(jnp.exp(scores - top), axis=-1, keepdims=True))
        probs = jnp.exp(scores - log_total).astype(jnp.bfloat16)
        return (matmul(probs, v_head).astype(jnp.bfloat16), log_total[:, 0])

    mixed, log_total = lax.map(one_head, jnp.arange(H, dtype=jnp.int32))
    return (join_heads(mixed), log_total)


def attend_bin_back(packed):
    query, key_rows, value, d_mixed, log_total, segment = packed
    mask = segment[:, None] == segment[None, :]
    scale = HD ** (-0.5)

    def one_head(head_index):
        q_head = head_slice(query, head_index)
        k_head = head_slice(key_rows, head_index)
        v_head = head_slice(value, head_index)
        d_head = head_slice(d_mixed, head_index)
        total_head = lax.dynamic_index_in_dim(log_total, head_index, 0, keepdims=False)
        scores = jnp.where(mask, matmul_right_t(q_head, k_head) * scale, masked_score)
        probs = jnp.exp(scores - total_head[:, None])
        d_probs = matmul_right_t(d_head, v_head)
        d_value = matmul_left_t(probs.astype(jnp.bfloat16), d_head)
        inner = jnp.sum(probs * d_probs, axis=-1, keepdims=True)
        d_scores = (probs * (d_probs - inner)).astype(jnp.bfloat16)
        d_query = matmul(d_scores, k_head) * scale
        d_key = matmul_left_t(d_scores, q_head) * scale
        return (d_query, d_key, d_value)

    d_query, d_key, d_value = lax.map(one_head, jnp.arange(H, dtype=jnp.int32))
    return (join_heads(d_query), join_heads(d_key), join_heads(d_value))


def square_sums(pieces):
    freq_sq = jnp.sum(pieces[12] * pieces[12])
    other_sq = jnp.float32(0.0)
    for member in pieces[:12]:
        other_sq = other_sq + jnp.sum(member * member)
    return (freq_sq, other_sq)


def shards(
    tokens,
    image_table,
    ln1_gain,
    ln1_bias,
    qkv_weight,
    qkv_bias,
    out_weight,
    out_bias,
    ln2_gain,
    ln2_bias,
    fc1_weight,
    fc1_bias,
    fc2_weight,
    fc2_bias,
    frequencies,
    cotangent,
):
    block_parameters = (
        lax.all_gather(ln1_gain, "fsdp", axis=0, tiled=True),
        lax.all_gather(ln1_bias, "fsdp", axis=0, tiled=True),
        lax.all_gather(qkv_weight, "fsdp", axis=0, tiled=True),
        lax.all_gather(qkv_bias, "fsdp", axis=0, tiled=True),
        lax.all_gather(out_weight, "fsdp", axis=0, tiled=True),
        lax.all_gather(out_bias, "fsdp", axis=0, tiled=True),
        lax.all_gather(ln2_gain, "fsdp", axis=0, tiled=True),
        lax.all_gather(ln2_bias, "fsdp", axis=0, tiled=True),
        lax.all_gather(fc1_weight, "fsdp", axis=0, tiled=True),
        lax.all_gather(fc1_bias, "fsdp", axis=0, tiled=True),
        lax.all_gather(fc2_weight, "fsdp", axis=0, tiled=True),
        lax.all_gather(fc2_bias, "fsdp", axis=0, tiled=True),
        lax.all_gather(frequencies, "fsdp", axis=0, tiled=True),
    )
    row_count, width = tokens.shape
    bin_count = row_count // BIN
    half_head = HD // 2
    segment, grid_row, grid_col = image_layout(image_table, bin_count, BIN)
    cosine, sine = rotary_tables(block_parameters[12], grid_row, grid_col)
    input_single_precision = tokens.astype(jnp.float32)
    first_centered_normalized, first_inverse_deviation = layer_norm_forward(input_single_precision)
    first_activation = (
        first_centered_normalized * block_parameters[0].astype(jnp.float32)
        + block_parameters[1].astype(jnp.float32)
    ).astype(jnp.bfloat16)
    qkv_full = matmul(first_activation, block_parameters[2]) + block_parameters[3].astype(
        jnp.float32
    )
    q_rot = rotate(qkv_full[:, :width].reshape(row_count, H, HD), cosine, sine)
    k_rot = rotate(qkv_full[:, width : 2 * width].reshape(row_count, H, HD), cosine, sine)
    q_low = q_rot.reshape(row_count, width).astype(jnp.bfloat16)
    k_low = k_rot.reshape(row_count, width).astype(jnp.bfloat16)
    v_low = qkv_full[:, 2 * width :].astype(jnp.bfloat16)
    q_bins = q_low.reshape(bin_count, BIN, width)
    k_bins = k_low.reshape(bin_count, BIN, width)
    v_bins = v_low.reshape(bin_count, BIN, width)
    mixed, log_total = lax.map(attend_bin, (q_bins, k_bins, v_bins, segment))
    mixed = mixed.reshape(row_count, width)
    residual_stream = (
        input_single_precision
        + matmul(mixed, block_parameters[4])
        + block_parameters[5].astype(jnp.float32)
    )
    second_centered_normalized, second_inverse_deviation = layer_norm_forward(residual_stream)
    second_activation = (
        second_centered_normalized * block_parameters[6].astype(jnp.float32)
        + block_parameters[7].astype(jnp.float32)
    ).astype(jnp.bfloat16)
    up_proj = matmul(second_activation, block_parameters[8]) + block_parameters[9].astype(
        jnp.float32
    )
    gelu_low = jax.nn.gelu(up_proj, approximate=False).astype(jnp.bfloat16)
    block_out = (
        residual_stream
        + matmul(gelu_low, block_parameters[10])
        + block_parameters[11].astype(jnp.float32)
    ).astype(jnp.bfloat16)
    block_parameters = (
        lax.all_gather(ln1_gain, "fsdp", axis=0, tiled=True),
        lax.all_gather(ln1_bias, "fsdp", axis=0, tiled=True),
        lax.all_gather(qkv_weight, "fsdp", axis=0, tiled=True),
        lax.all_gather(qkv_bias, "fsdp", axis=0, tiled=True),
        lax.all_gather(out_weight, "fsdp", axis=0, tiled=True),
        lax.all_gather(out_bias, "fsdp", axis=0, tiled=True),
        lax.all_gather(ln2_gain, "fsdp", axis=0, tiled=True),
        lax.all_gather(ln2_bias, "fsdp", axis=0, tiled=True),
        lax.all_gather(fc1_weight, "fsdp", axis=0, tiled=True),
        lax.all_gather(fc1_bias, "fsdp", axis=0, tiled=True),
        lax.all_gather(fc2_weight, "fsdp", axis=0, tiled=True),
        lax.all_gather(fc2_bias, "fsdp", axis=0, tiled=True),
        lax.all_gather(frequencies, "fsdp", axis=0, tiled=True),
    )
    output_gradient = cotangent.astype(jnp.float32)
    fc2_bias_grad = jnp.sum(output_gradient, axis=0)
    fc2_weight_grad = matmul_left_t(gelu_low, cotangent)
    d_up = (matmul_right_t(cotangent, block_parameters[10]) * gelu_slope(up_proj)).astype(
        jnp.bfloat16
    )
    fc1_bias_grad = jnp.sum(d_up.astype(jnp.float32), axis=0)
    fc1_weight_grad = matmul_left_t(second_activation, d_up)
    second_activation_gradient = matmul_right_t(d_up, block_parameters[8])
    second_norm_gain_gradient = jnp.sum(
        second_activation_gradient * second_centered_normalized, axis=0
    )
    ln2_bias_grad = jnp.sum(second_activation_gradient, axis=0)
    residual_gradient = output_gradient + layer_norm_backward(
        second_activation_gradient,
        second_centered_normalized,
        second_inverse_deviation,
        block_parameters[6].astype(jnp.float32),
    )
    d_att = residual_gradient.astype(jnp.bfloat16)
    out_bias_grad = jnp.sum(d_att.astype(jnp.float32), axis=0)
    out_weight_grad = matmul_left_t(mixed, d_att)
    d_mixed = matmul_right_t(d_att, block_parameters[4]).astype(jnp.bfloat16)
    d_qrot, d_krot, d_value = lax.map(
        attend_bin_back,
        (q_bins, k_bins, v_bins, d_mixed.reshape(bin_count, BIN, width), log_total, segment),
    )
    d_qrot = d_qrot.reshape(row_count, H, HD)
    d_krot = d_krot.reshape(row_count, H, HD)
    d_theta = (
        d_qrot[..., half_head:] * q_rot[..., :half_head]
        - d_qrot[..., :half_head] * q_rot[..., half_head:]
    )
    d_theta = (
        d_theta
        + d_krot[..., half_head:] * k_rot[..., :half_head]
        - d_krot[..., :half_head] * k_rot[..., half_head:]
    )
    frequencies_grad = jnp.concatenate(
        [
            jnp.sum(grid_row[:, None, None] * d_theta, axis=0).reshape(-1),
            jnp.sum(grid_col[:, None, None] * d_theta, axis=0).reshape(-1),
        ]
    )
    d_query = rotate(d_qrot, cosine, -sine).reshape(row_count, width)
    d_key = rotate(d_krot, cosine, -sine).reshape(row_count, width)
    d_qkv = jnp.concatenate([d_query, d_key, d_value.reshape(row_count, width)], axis=1).astype(
        jnp.bfloat16
    )
    qkv_bias_grad = jnp.sum(d_qkv.astype(jnp.float32), axis=0)
    qkv_weight_grad = matmul_left_t(first_activation, d_qkv)
    first_activation_gradient = matmul_right_t(d_qkv, block_parameters[2])
    first_norm_gain_gradient = jnp.sum(
        first_activation_gradient * first_centered_normalized, axis=0
    )
    ln1_bias_grad = jnp.sum(first_activation_gradient, axis=0)
    tokens_grad = (
        residual_gradient
        + layer_norm_backward(
            first_activation_gradient,
            first_centered_normalized,
            first_inverse_deviation,
            block_parameters[0].astype(jnp.float32),
        )
    ).astype(jnp.bfloat16)
    pieces = (
        lax.psum_scatter(first_norm_gain_gradient, "fsdp", scatter_dimension=0, tiled=True),
        lax.psum_scatter(ln1_bias_grad, "fsdp", scatter_dimension=0, tiled=True),
        lax.psum_scatter(qkv_weight_grad, "fsdp", scatter_dimension=0, tiled=True),
        lax.psum_scatter(qkv_bias_grad, "fsdp", scatter_dimension=0, tiled=True),
        lax.psum_scatter(out_weight_grad, "fsdp", scatter_dimension=0, tiled=True),
        lax.psum_scatter(out_bias_grad, "fsdp", scatter_dimension=0, tiled=True),
        lax.psum_scatter(second_norm_gain_gradient, "fsdp", scatter_dimension=0, tiled=True),
        lax.psum_scatter(ln2_bias_grad, "fsdp", scatter_dimension=0, tiled=True),
        lax.psum_scatter(fc1_weight_grad, "fsdp", scatter_dimension=0, tiled=True),
        lax.psum_scatter(fc1_bias_grad, "fsdp", scatter_dimension=0, tiled=True),
        lax.psum_scatter(fc2_weight_grad, "fsdp", scatter_dimension=0, tiled=True),
        lax.psum_scatter(fc2_bias_grad, "fsdp", scatter_dimension=0, tiled=True),
        lax.psum_scatter(frequencies_grad, "fsdp", scatter_dimension=0, tiled=True),
    )
    pieces = (
        lax.psum(pieces[0].astype(jnp.bfloat16), "dp").astype(jnp.float32),
        lax.psum(pieces[1].astype(jnp.bfloat16), "dp").astype(jnp.float32),
        lax.psum(pieces[2].astype(jnp.bfloat16), "dp").astype(jnp.float32),
        lax.psum(pieces[3].astype(jnp.bfloat16), "dp").astype(jnp.float32),
        lax.psum(pieces[4].astype(jnp.bfloat16), "dp").astype(jnp.float32),
        lax.psum(pieces[5].astype(jnp.bfloat16), "dp").astype(jnp.float32),
        lax.psum(pieces[6].astype(jnp.bfloat16), "dp").astype(jnp.float32),
        lax.psum(pieces[7].astype(jnp.bfloat16), "dp").astype(jnp.float32),
        lax.psum(pieces[8].astype(jnp.bfloat16), "dp").astype(jnp.float32),
        lax.psum(pieces[9].astype(jnp.bfloat16), "dp").astype(jnp.float32),
        lax.psum(pieces[10].astype(jnp.bfloat16), "dp").astype(jnp.float32),
        lax.psum(pieces[11].astype(jnp.bfloat16), "dp").astype(jnp.float32),
        lax.psum(pieces[12].astype(jnp.bfloat16), "dp").astype(jnp.float32),
    )
    freq_sq, other_sq = square_sums(pieces)
    freq_sq, other_sq = lax.psum((freq_sq, other_sq), "fsdp")
    return (
        block_out,
        tokens_grad,
        pieces[0],
        pieces[1],
        pieces[2],
        pieces[3],
        pieces[4],
        pieces[5],
        pieces[6],
        pieces[7],
        pieces[8],
        pieces[9],
        pieces[10],
        pieces[11],
        pieces[12],
        jnp.sqrt(freq_sq),
        jnp.sqrt(other_sq),
    )


def solution(mesh):
    placed = (
        P(("fsdp", "dp"), None),
        P(("fsdp", "dp"), None),
        P("fsdp"),
        P("fsdp"),
        P("fsdp", None),
        P("fsdp"),
        P("fsdp", None),
        P("fsdp"),
        P("fsdp"),
        P("fsdp"),
        P("fsdp", None),
        P("fsdp"),
        P("fsdp", None),
        P("fsdp"),
        P("fsdp"),
        P(("fsdp", "dp"), None),
    )
    return jax.shard_map(
        shards,
        mesh=mesh,
        in_specs=placed,
        out_specs=(
            P(("fsdp", "dp"), None),
            P(("fsdp", "dp"), None),
            P("fsdp"),
            P("fsdp"),
            P("fsdp", None),
            P("fsdp"),
            P("fsdp", None),
            P("fsdp"),
            P("fsdp"),
            P("fsdp"),
            P("fsdp", None),
            P("fsdp"),
            P("fsdp", None),
            P("fsdp"),
            P("fsdp"),
            P(),
            P(),
        ),
        check_vma=False,
    )
```

profile of v0, /device:TPU:0, one launch (start us, length us, event | category | flops | bytes accessed | tf_op | source)
XLA Modules:
  0.0 1132.7 jit_solution(17472799987714436141)
XLA Ops:
  19.5 40.6 %all-reduce.19 = (bf16[768]{0:T(1024)(128)(2,1)S(1)}, bf16[2304]{0:T(1024)(128)(2,1)S(1)}, bf16[768]{0:T(1024)(128)(2,1)S(1)}, bf16[768]{0:T(1024)(128)(2,1)S(1)...) all-reduce(bf16[768]{0:T(1024)(128)(2,1)S(1)} %dynamic-update-slice, ...), channel_id=1, replica_groups=mesh['fsdp'=8,'dp'=4] {'fsdp'}, use_global_device_ids=true, to_apply=%add.3 | all-reduce | flops 7680 | bytes 30720
  62.9 26.9 %all-gather = bf16[8,1,384]{2,1,0:T(2,128)(2,1)S(1)} all-gather(bf16[1,1,384]{2,1,0:T(2,128)(2,1)S(1)} %reshape.697), channel_id=1, replica_groups=mesh['fsdp'=8,'dp'=4] {'fsdp'}, dimensions={0}, use_global_device_ids=true | all-gather | bytes 6912 | tf_op jit(solution)/shard_map/all_gather | solution.py:183
  91.9 6.3 convolution_add_fusion
  109.7 10.8 fusion.87
  126.9 83.8 %while.48 = (s32[]{:T(128)}, bf16[12,1024,64]{1,2,0:T(8,128)(2,1)}, f32[12,1024]{1,0:T(8,128)S(1)}, s32[12]{0:T(128)S(1)}, bf16[1024,768]{1,0:T(8,128)(2,1)S(1)}...) while((s32[]{:T(128)}, bf16[12,1024,64]{1,2,0:T(8,128)(2,1)}, ...), condition=%wide.region_9.10_spmd.clone, body=%wide.region_6.9_spmd.clone.sunk | while | flops 283180032 | bytes 13558979 | solution.py:118
  216.8 50.6 %fusion.44 = (bf16[1024,3072]{1,0:T(8,128)(2,1)}, f32[1024,3072]{1,0:T(8,128)}) fusion(f32[3072]{0:T(1024)S(1)} %bitcast.103, bf16[768,3072]{1,0:T(8,128)(2,1)} %all-gather.10.cloned.1.call-done, f32[1024,768]{0,1:T(8,128)} %copy-done.4, f32[768]{0:T(1024)S(1)} %convert_element_type.206, f32[768]{0:T(1024)S(1)} %convert_element_type.205, ...), kind=kOutput, calls=%fused_computation.50 | convolution fusion | flops 5043388416 | bytes 26765312 | tf_op jit(solution)/shard_map/dot_general | solution.py:15
  267.4 13.0 %all-gather.12.cloned.1.call-done = bf16[3072,768]{1,0:T(8,128)(2,1)} async-done(((bf16[384,768]{1,0:T(8,128)(2,1)}), bf16[3072,768]{1,0:T(8,128)(2,1)}) %all-gather.12.cloned.1.call-update) | async-done | bytes 4718608 | tf_op jit(solution)/shard_map/all_gather | solution.py:184
  280.4 11.9 %convert_reduce_fusion = (f32[3072]{0:T(1024)S(1)}, bf16[1024,3072]{1,0:T(8,128)(2,1)S(1)}) fusion(f32[1024,3072]{1,0:T(8,128)} %get-tuple-element.504, f32[3072]{0:T(1024)S(1)} %bitcast.104, bf16[1024,768]{1,0:T(8,128)(2,1)S(1)} %copy-done.15, bf16[3072,768]{1,0:T(8,128)(2,1)} %all-gather.12.cloned.1.call-done), kind=kOutput, calls=%fused_computation.57 | convolution fusion | flops 4872729600 | bytes 25190400 | tf_op jit(solution)/shard_map/dot_general | solution.py:25
  292.3 6.7 fusion.100
  317.1 230.8 %while.49 = (s32[]{:T(128)}, f32[12,1024,64]{1,2,0:T(8,128)}, f32[12,1024,64]{1,2,0:T(8,128)}, bf16[12,1024,64]{1,2,0:T(8,128)(2,1)}, s32[12]{0:T(128)S(1)}, /*i...) while((s32[]{:T(128)}, f32[12,1024,64]{1,2,0:T(8,128)}, ...), condition=%wide.region_16.17_spmd.clone, body=%wide.region_14.16_spmd.clone.sunk | while | flops 681704448 | bytes 50886960 | solution.py:143
  547.9 12.2 %multiply_subtract_fusion = (f32[1024,12,32]{0,2,1:T(8,128)S(1)}, bf16[1024,12,32]{0,2,1:T(8,128)(2,1)S(1)}, bf16[1024,12,32]{0,2,1:T(8,128)(2,1)S(1)}, bf16[1024,12,32]{0,2,1:T(8,128)(2,1)S(1)}) fusion(f32[1024,12,64]{0,2,1:T(8,128)} %bitcast.87, f32[1024,12,64]{0,2,1:T(8,128)} %bitcast.97, f32[1024,12,64]{0,2,1:T(8,128)} %bitcast.86, ...), kind=kLoop, calls=%fused_computation.114 | loop fusion | flops 13762560 | bytes 16526336 | tf_op jit(solution)/shard_map/sub | solution.py:280
  560.2 6.4 multiply_reduce_fusion.7
  569.1 7.0 fusion.89
  576.2 10.6 fusion.93
  586.8 9.9 fusion.101
  599.3 10.1 add_convert_fusion
  612.1 8.6 fusion.99
  636.2 35.3 %all-reduce.18 = (bf16[768]{0:T(1024)(128)(2,1)S(1)}, bf16[768]{0:T(1024)(128)(2,1)S(1)}, bf16[2304]{0:T(1024)(128)(2,1)S(1)}, bf16[768]{0:T(1024)(128)(2,1)S(1)...) all-reduce(f32[768]{0:T(1024)S(1)} %get-tuple-element.365, ...), channel_id=2, replica_groups=mesh['fsdp'=8,'dp'=4] {'fsdp'}, use_global_device_ids=true, to_apply=%region_20.21.clone | all-reduce | flops 10752 | bytes 64512
  672.2 6.1 all-reduce.20
  686.8 18.9 %reduce-scatter.5.cloned.1.call-done = f32[96,2304]{1,0:T(8,128)} async-done(((f32[768,2304]{1,0:T(8,128)}), f32[96,2304]{1,0:T(8,128)}) %reduce-scatter.5.cloned.1.call-update) | async-done | bytes 884752 | tf_op jit(solution)/shard_map/reduce_scatter | solution.py:314
  707.7 162.8 %reduce-scatter.9.cloned.1.call-done = f32[96,3072]{1,0:T(8,128)} async-done(((f32[768,3072]{1,0:T(8,128)}), f32[96,3072]{1,0:T(8,128)}) %reduce-scatter.9.cloned.1.call-update) | async-done | bytes 1179664 | tf_op jit(solution)/shard_map/reduce_scatter | solution.py:320
  872.6 162.7 %reduce-scatter.11.cloned.1.call-done = f32[384,768]{1,0:T(8,128)} async-done(((f32[3072,768]{1,0:T(8,128)}), f32[384,768]{1,0:T(8,128)}) %reduce-scatter.11.cloned.1.call-update) | async-done | bytes 1179664 | tf_op jit(solution)/shard_map/reduce_scatter | solution.py:322
  1042.2 42.1 %all-reduce.24.cloned.1.call-done = (bf16[96,2304]{1,0:T(8,128)(2,1)}, bf16[96,768]{1,0:T(8,128)(2,1)}, bf16[96,3072]{1,0:T(8,128)(2,1)}, bf16[384,768]{1,0:T(8,128)(2,1)}) async-done(((bf16[96,2304]{1,0:T(8,128)(2,1)}, bf16[96,768]{1,0:T(8,128)(2,1)}, bf16[96,3072]{1,0:T(8,128)(2,1)}, bf16[384,768]{1,0:T(8,128)(2,1)}), (bf16[96,2304]{1,0:T(8,128)(2,1)}, bf16[96,768]{1,0:T(8,128)(2,1)}, ...) | async-done | bytes 1769488 | tf_op jit(solution)/shard_map/psum | solution.py:329
  1100.3 22.0 %all-reduce.17 = (f32[]{:T(128)}, f32[]{:T(128)}) all-reduce(f32[]{:T(128)} %get-tuple-element.469, f32[]{:T(128)S(6)} %add.305), channel_id=1, replica_groups=mesh['fsdp'=8,'dp'=4] {'fsdp'}, use_global_device_ids=true, to_apply=%region_56.57 | all-reduce | flops 2 | bytes 16 | tf_op jit(solution)/shard_map/psum | solution.py:342
  (396 shorter events, 381.4 us)
Async XLA Ops:
  7.2 84.7 %all-gather.6.cloned.1.call-start = ((), (), s32[]{:S(2)}) async-start(), calls=%async_computation.4 | async-start | bytes 3981312 | tf_op jit(solution)/shard_map/all_gather | solution.py:176
  7.9 202.8 %all-gather.8.cloned.1.call-start = ((), (), s32[]{:S(2)}) async-start(), calls=%async_computation.5 | async-start | bytes 1327104 | tf_op jit(solution)/shard_map/all_gather | solution.py:178
  8.7 208.1 %all-gather.10.cloned.1.call-start = ((), (), s32[]{:S(2)}) async-start(), calls=%async_computation.6 | async-start | bytes 5308416 | tf_op jit(solution)/shard_map/all_gather | solution.py:182
  9.4 271.0 %all-gather.12.cloned.1.call-start = ((), (), s32[]{:S(2)}) async-start(), calls=%async_computation.7 | async-start | bytes 5308416 | tf_op jit(solution)/shard_map/all_gather | solution.py:184
  10.0 675.2 %reduce-scatter.7.cloned.1.call-start = ((), (), s32[]{:S(2)}) async-start(), calls=%async_computation.9 | async-start | bytes 2654208 | tf_op jit(solution)/shard_map/reduce_scatter | solution.py:316
  60.1 29.8 %copy-start.14 = (bf16[1024,768]{1,0:T(8,128)(2,1)S(1)}, bf16[1024,768]{1,0:T(8,128)(2,1)}, u32[]{:S(2)}) copy-start(bf16[1024,768]{1,0:T(8,128)(2,1)} %param.35) | copy-start | bytes 4718596
  61.9 148.8 %copy-start.1 = (bf16[1024,768]{0,1:T(8,128)(2,1)}, bf16[1024,768]{0,1:T(8,128)(2,1)S(1)}, u32[]{:S(2)}) copy-start(bf16[1024,768]{0,1:T(8,128)(2,1)S(1)} %copy.80) | copy-start | bytes 4718596
  61.9 29.9 %copy-start.32 = (f32[768]{0:T(1024)}, f32[768]{0:T(1024)S(1)}, u32[]{:S(2)}) copy-start(f32[768]{0:T(1024)S(1)} %convert_element_type.195) | copy-start | bytes 9220
  62.0 29.9 %copy-start.28 = (f32[768]{0:T(1024)}, f32[768]{0:T(1024)S(1)}, u32[]{:S(2)}) copy-start(f32[768]{0:T(1024)S(1)} %convert_element_type.194) | copy-start | bytes 9220
  62.2 36.0 %copy-start.22 = (f32[1024]{0:T(1024)}, f32[1024]{0:T(1024)S(1)}, u32[]{:S(2)}) copy-start(f32[1024]{0:T(1024)S(1)} %broadcast_multiply_fusion.5) | copy-start | bytes 12292
  62.7 35.5 %copy-start.30 = (f32[1024]{0:T(1024)}, f32[1024]{0:T(1024)S(1)}, u32[]{:S(2)}) copy-start(f32[1024]{0:T(1024)S(1)} %add_rsqrt_fusion.1) | copy-start | bytes 12292
  62.8 46.8 %copy-start.18 = (f32[12,32]{1,0:T(8,128)}, f32[12,32]{1,0:T(8,128)S(1)}, u32[]{:S(2)}) copy-start(f32[12,32]{1,0:T(8,128)S(1)} %slice.81) | copy-start | bytes 4612
  62.9 46.7 %copy-start.20 = (f32[12,32]{1,0:T(8,128)}, f32[12,32]{1,0:T(8,128)S(1)}, u32[]{:S(2)}) copy-start(f32[12,32]{1,0:T(8,128)S(1)} %slice.79) | copy-start | bytes 4612
  91.8 17.8 %copy-start.24 = (f32[1024]{0:T(1024)}, f32[1024]{0:T(1024)S(1)}, u32[]{:S(2)}) copy-start(f32[1024]{0:T(1024)S(1)} %get-tuple-element.490) | copy-start | bytes 12292
  216.8 63.6 %copy-start.15 = (bf16[1024,768]{1,0:T(8,128)(2,1)S(1)}, bf16[1024,768]{1,0:T(8,128)(2,1)}, u32[]{:S(2)}) copy-start(bf16[1024,768]{1,0:T(8,128)(2,1)} %param.35) | copy-start | bytes 4718596
  312.4 393.3 %reduce-scatter.5.cloned.1.call-start = ((), (), s32[]{:S(2)}) async-start(), calls=%async_computation.8 | async-start | bytes 7962624 | tf_op jit(solution)/shard_map/reduce_scatter | solution.py:314
  317.1 230.8 %copy-start.3 = (f32[1024,768]{0,1:T(8,128)S(1)}, f32[1024,768]{0,1:T(8,128)}, u32[]{:S(2)}) copy-start(f32[1024,768]{0,1:T(8,128)} %copy.82) | copy-start | bytes 9437188
  317.1 230.8 %copy-start.19 = (f32[12,32]{1,0:T(8,128)S(1)}, f32[12,32]{1,0:T(8,128)}, u32[]{:S(2)}) copy-start(f32[12,32]{1,0:T(8,128)} %copy-done.18) | copy-start | bytes 4612
  317.1 230.8 %copy-start.21 = (f32[12,32]{1,0:T(8,128)S(1)}, f32[12,32]{1,0:T(8,128)}, u32[]{:S(2)}) copy-start(f32[12,32]{1,0:T(8,128)} %copy-done.20) | copy-start | bytes 4612
  317.1 230.8 %copy-start.25 = (f32[1024]{0:T(1024)S(1)}, f32[1024]{0:T(1024)}, u32[]{:S(2)}) copy-start(f32[1024]{0:T(1024)} %copy-done.24) | copy-start | bytes 12292
  317.1 230.8 %copy-start.27 = (f32[1024]{0:T(1024)S(1)}, f32[1024]{0:T(1024)}, u32[]{:S(2)}) copy-start(f32[1024]{0:T(1024)} %copy-done.26) | copy-start | bytes 12292
  576.1 294.4 %reduce-scatter.9.cloned.1.call-start = ((), (), s32[]{:S(2)}) async-start(), calls=%async_computation.10 | async-start | bytes 10616832 | tf_op jit(solution)/shard_map/reduce_scatter | solution.py:320
  586.8 448.6 %reduce-scatter.11.cloned.1.call-start = ((), (), s32[]{:S(2)}) async-start(), calls=%async_computation.11 | async-start | bytes 10616832 | tf_op jit(solution)/shard_map/reduce_scatter | solution.py:322
  596.7 487.6 %all-reduce.24.cloned.1.call-start = ((), (), s32[]{:S(2)}) async-start(), calls=%async_computation.12 | async-start | bytes 3538944 | tf_op jit(solution)/shard_map/psum | solution.py:329
  (37 other events, 154.8 us)
Sparse Core Ops, SparseCore 0:
  10.2 67.9 all-gather.5
  80.3 39.9 all-gather.7
  122.6 78.0 all-gather.9
  202.7 77.6 all-gather.11
  312.5 68.1 reduce-scatter.6
  576.2 129.4 reduce-scatter.4
  709.3 161.1 reduce-scatter.8
  874.1 161.1 reduce-scatter.10
  1039.1 45.1 all-reduce.23
where the time goes:
time: 1140 us; the launch traced here: 1130 us
  waiting for transfers between devices  402 us (35%)
  matrix products  366 us (32%)
  blocking collectives  131 us (11%)
  other arithmetic  101 us (9%)
  local copies, waits for them, and re-layouts  62 us (5%)
  loops' own time  40.6 us (4%)
  between operations  29.2 us (3%)
    reduce_scatter x1, waiting for transfers between devices, shards(): lax.psum_scatter(fc1_weight_grad, 'fsdp', scatter_dimension=0, tiled=True)  163 us
    reduce_scatter x1, waiting for transfers between devices, shards(): lax.psum_scatter(fc2_weight_grad, 'fsdp', scatter_dimension=0, tiled=True)  163 us
    dot_general x40, matrix products, matmul_right_t(): lax.dot_general(left, right, (((1,), (1,)), ((), ())), preferred_element_...  145 us
    dot_general x28, matrix products, matmul(): return jnp.dot(left, right, preferred_element_type=jnp.float32)  132 us
    dot_general x28, matrix products, matmul_left_t(): lax.dot_general(left, right, (((0,), (0,)), ((), ())), preferred_element_...  89.3 us
    unnamed x2, blocking collectives  75.9 us
    psum x1, waiting for transfers between devices, shards(): lax.psum(pieces[2].astype(jnp.bfloat16), 'dp').astype(jnp.float32)  42.1 us
    another operation x1, loops' own time, attend_bin_back(): d_query, d_key, d_value = lax.map(one_head, jnp.arange(H, dtype=jnp.int32))  32.2 us
  transfers between devices with their start and end apart: 9, of which 5 were waited for; matrix products, arithmetic and copies ran while one was open for 42% of the time, Pallas kernels for 0%

commit v1 on v0

--- a/solution.py
+++ b/solution.py
@@ -9,6 +9,18 @@
 norm_eps = 1e-06
 masked_score = -1e30
 inv_sqrt_two_pi = 0.3989422804014327
+
+
+def doubled_up(array, axis, dim):
+    ways, here, lap = (lax.axis_size(axis), lax.axis_index(axis), array.shape[dim])
+    line, have = (array, 1)
+    while have < ways:
+        line = jnp.concatenate(
+            [line, lax.ppermute(line, axis, [(d, (d - have) % ways) for d in range(ways)])],
+            axis=dim,
+        )
+        have = 2 * have
+    return jnp.roll(line, here * lap, axis=dim)
 
 
 def matmul(left, right):
@@ -181,7 +193,7 @@
         lax.all_gather(ln2_bias, "fsdp", axis=0, tiled=True),
         lax.all_gather(fc1_weight, "fsdp", axis=0, tiled=True),
         lax.all_gather(fc1_bias, "fsdp", axis=0, tiled=True),
-        lax.all_gather(fc2_weight, "fsdp", axis=0, tiled=True),
+        doubled_up(fc2_weight, "fsdp", 0),
         lax.all_gather(fc2_bias, "fsdp", axis=0, tiled=True),
         lax.all_gather(frequencies, "fsdp", axis=0, tiled=True),
     )

time: 1140 us -> 1240 us (1.088)
  waiting for transfers between devices: 402 us -> 484 us
  local copies, waits for them, and re-layouts: 62 us -> 77 us
    ppermute x0 -> x3, waiting for transfers between devices: none -> 251 us  [doubled_up(): lax.ppermute(line, axis, [(d, (d - have) % ways) for d in range(ways)])]
    reduce_scatter x1, waiting for transfers between devices: 163 us -> 12.4 us  [shards(): lax.psum_scatter(fc1_weight_grad, 'fsdp', scatter_dimension=0, tiled=True)]
    reduce_scatter x1, waiting for transfers between devices: 18.9 us -> 0.01 us  [shards(): lax.psum_scatter(qkv_weight_grad, 'fsdp', scatter_dimension=0, tiled=True)]
    unnamed x113 -> x128, local copies, waits for them, and re-layouts: 28 us -> 39.4 us
  transfers between devices with their start and end apart: 9 -> 12, of which waited for: 5 -> 7; matrix products, arithmetic and copies ran while one was open for 42% -> 40% of each run, Pallas kernels for 0% -> 0%
where the time goes in v1:
time: 1240 us
  waiting for transfers between devices  484 us (39%)
  matrix products  369 us (30%)
  blocking collectives  130 us (10%)
  other arithmetic  101 us (8%)
  local copies, waits for them, and re-layouts  77 us (6%)
  loops' own time  40.6 us (3%)
  between operations  29.3 us (2%)
    ppermute x3, waiting for transfers between devices, doubled_up(): lax.ppermute(line, axis, [(d, (d - have) % ways) for d in range(ways)])  251 us
    reduce_scatter x1, waiting for transfers between devices, shards(): lax.psum_scatter(fc2_weight_grad, 'fsdp', scatter_dimension=0, tiled=True)  163 us
    dot_general x40, matrix products, matmul_right_t(): lax.dot_general(left, right, (((1,), (1,)), ((), ())), preferred_element_...  147 us
    dot_general x28, matrix products, matmul(): return jnp.dot(left, right, preferred_element_type=jnp.float32)  131 us
    dot_general x28, matrix products, matmul_left_t(): lax.dot_general(left, right, (((0,), (0,)), ((), ())), preferred_element_...  91.2 us
    unnamed x2, blocking collectives  74.8 us
    psum x1, waiting for transfers between devices, shards(): lax.psum(pieces[2].astype(jnp.bfloat16), 'dp').astype(jnp.float32)  42.2 us
    unnamed x128, local copies, waits for them, and re-layouts  39.4 us
  transfers between devices with their start and end apart: 12, of which 7 were waited for; matrix products, arithmetic and copies ran while one was open for 40% of the time, Pallas kernels for 0%

profile of v1, /device:TPU:0, one launch (start us, length us, event | category | flops | bytes accessed | tf_op | source)
XLA Modules:
  0.0 1235.8 jit_solution(14556381745924785482)
XLA Ops:
  19.5 40.6 %all-reduce.19 = (bf16[768]{0:T(1024)(128)(2,1)S(1)}, bf16[2304]{0:T(1024)(128)(2,1)S(1)}, bf16[768]{0:T(1024)(128)(2,1)S(1)}, bf16[768]{0:T(1024)(128)(2,1)S(1)...) all-reduce(bf16[768]{0:T(1024)(128)(2,1)S(1)} %dynamic-update-slice, ...), channel_id=1, replica_groups=mesh['fsdp'=8,'dp'=4] {'fsdp'}, use_global_device_ids=true, to_apply=%add.3 | all-reduce | flops 7680 | bytes 30720
  62.9 26.9 %all-gather = bf16[8,1,384]{2,1,0:T(2,128)(2,1)S(1)} all-gather(bf16[1,1,384]{2,1,0:T(2,128)(2,1)S(1)} %reshape.697), channel_id=1, replica_groups=mesh['fsdp'=8,'dp'=4] {'fsdp'}, dimensions={0}, use_global_device_ids=true | all-gather | bytes 6912 | tf_op jit(solution)/shard_map/all_gather | solution.py:195
  109.9 10.8 fusion.92
  127.2 83.8 %while.48 = (s32[]{:T(128)}, bf16[12,1024,64]{1,2,0:T(8,128)(2,1)}, f32[12,1024]{1,0:T(8,128)S(1)}, s32[12]{0:T(128)S(1)}, bf16[1024,768]{1,0:T(8,128)(2,1)S(1)}...) while((s32[]{:T(128)}, bf16[12,1024,64]{1,2,0:T(8,128)(2,1)}, ...), condition=%wide.region_9.10_spmd.clone, body=%wide.region_6.9_spmd.clone.sunk | while | flops 283180032 | bytes 13559479 | solution.py:130
  217.1 50.6 %fusion.44 = (bf16[1024,3072]{1,0:T(8,128)(2,1)}, f32[1024,3072]{1,0:T(8,128)}) fusion(f32[3072]{0:T(1024)S(1)} %bitcast.99, bf16[768,3072]{1,0:T(8,128)(2,1)} %all-gather.10.cloned.1.call-done, f32[1024,768]{0,1:T(8,128)} %copy-done.4, f32[768]{0:T(1024)S(1)} %convert_element_type.206, f32[768]{0:T(1024)S(1)} %convert_element_type.205, ...), kind=kOutput, calls=%fused_computation.50 | convolution fusion | flops 5043388416 | bytes 26765312 | tf_op jit(solution)/shard_map/dot_general | solution.py:27
  267.7 12.7 %all-gather.12.cloned.1.call-done = bf16[3072,768]{1,0:T(8,128)(2,1)} async-done(((bf16[384,768]{1,0:T(8,128)(2,1)}), bf16[3072,768]{1,0:T(8,128)(2,1)}) %all-gather.12.cloned.1.call-update) | async-done | bytes 4718608 | tf_op jit(solution)/shard_map/all_gather | solution.py:254
  280.5 11.9 convert_reduce_fusion
  292.4 6.7 fusion.105
  317.1 233.1 %while.49 = (s32[]{:T(128)}, f32[12,1024,64]{1,2,0:T(8,128)}, f32[12,1024,64]{1,2,0:T(8,128)}, bf16[12,1024,64]{1,2,0:T(8,128)(2,1)}, s32[12]{0:T(128)S(1)}, /*i...) while((s32[]{:T(128)}, f32[12,1024,64]{1,2,0:T(8,128)}, ...), condition=%wide.region_16.17_spmd.clone, body=%wide.region_14.16_spmd.clone.sunk | while | flops 681704448 | bytes 50888476 | solution.py:155
  550.2 12.1 multiply_subtract_fusion
  564.7 6.4 multiply_reduce_fusion.7
  572.5 8.4 fusion.94
  581.2 10.5 fusion.98
  593.1 10.1 fusion.106
  605.7 26.2 %collective-permute-done = bf16[384,768]{1,0:T(8,128)(2,1)S(1)} collective-permute-done((bf16[384,768]{1,0:T(8,128)(2,1)S(1)}, bf16[384,768]{1,0:T(8,128)(2,1)S(1)}, u32[]{:S(2)}, u32[]{:S(2)}) %collective-permute-start) | collective-permute-done | bytes 589856 | tf_op jit(solution)/shard_map/ppermute | solution.py:19
  632.9 50.1 %collective-permute-done.1 = bf16[768,768]{1,0:T(8,128)(2,1)S(1)} collective-permute-done((bf16[768,768]{1,0:T(8,128)(2,1)S(1)}, bf16[768,768]{1,0:T(8,128)(2,1)S(1)}, u32[]{:S(2)}, u32[]{:S(2)}) %collective-permute-start.1) | collective-permute-done | bytes 1179680 | tf_op jit(solution)/shard_map/ppermute | solution.py:19
  692.8 174.8 %collective-permute-done.2 = bf16[1536,768]{1,0:T(8,128)(2,1)} collective-permute-done((bf16[1536,768]{1,0:T(8,128)(2,1)}, bf16[1536,768]{1,0:T(8,128)(2,1)}, u32[]{:S(2)}, u32[]{:S(2)}) %collective-permute-start.2) | collective-permute-done | bytes 2359328 | tf_op jit(solution)/shard_map/ppermute | solution.py:19
  877.3 8.5 fusion.104
  893.3 34.2 %all-reduce.18 = (bf16[768]{0:T(1024)(128)(2,1)S(1)}, bf16[768]{0:T(1024)(128)(2,1)S(1)}, bf16[2304]{0:T(1024)(128)(2,1)S(1)}, bf16[768]{0:T(1024)(128)(2,1)S(1)...) all-reduce(f32[768]{0:T(1024)S(1)} %get-tuple-element.365, ...), channel_id=2, replica_groups=mesh['fsdp'=8,'dp'=4] {'fsdp'}, use_global_device_ids=true, to_apply=%region_20.21.clone | all-reduce | flops 10752 | bytes 64512
  933.6 9.1 add_convert_fusion
  961.2 12.4 %reduce-scatter.9.cloned.1.call-done = f32[96,3072]{1,0:T(8,128)} async-done(((f32[768,3072]{1,0:T(8,128)}), f32[96,3072]{1,0:T(8,128)}) %reduce-scatter.9.cloned.1.call-update) | async-done | bytes 1179664 | tf_op jit(solution)/shard_map/reduce_scatter | solution.py:332
  975.8 162.7 %reduce-scatter.11.cloned.1.call-done = f32[384,768]{1,0:T(8,128)} async-done(((f32[3072,768]{1,0:T(8,128)}), f32[384,768]{1,0:T(8,128)}) %reduce-scatter.11.cloned.1.call-update) | async-done | bytes 1179664 | tf_op jit(solution)/shard_map/reduce_scatter | solution.py:334
  1145.3 42.2 %all-reduce.24.cloned.1.call-done = (bf16[96,2304]{1,0:T(8,128)(2,1)}, bf16[96,768]{1,0:T(8,128)(2,1)}, bf16[96,3072]{1,0:T(8,128)(2,1)}, bf16[384,768]{1,0:T(8,128)(2,1)}) async-done(((bf16[96,2304]{1,0:T(8,128)(2,1)}, bf16[96,768]{1,0:T(8,128)(2,1)}, bf16[96,3072]{1,0:T(8,128)(2,1)}, bf16[384,768]{1,0:T(8,128)(2,1)}), (bf16[96,2304]{1,0:T(8,128)(2,1)}, bf16[96,768]{1,0:T(8,128)(2,1)}, ...) | async-done | bytes 1769488 | tf_op jit(solution)/shard_map/psum | solution.py:341
  1203.6 21.9 %all-reduce.17 = (f32[]{:T(128)}, f32[]{:T(128)}) all-reduce(f32[]{:T(128)} %get-tuple-element.469, f32[]{:T(128)S(6)} %add.317), channel_id=1, replica_groups=mesh['fsdp'=8,'dp'=4] {'fsdp'}, use_global_device_ids=true, to_apply=%region_56.57 | all-reduce | flops 2 | bytes 16 | tf_op jit(solution)/shard_map/psum | solution.py:354
  (420 shorter events, 416.0 us)
Async XLA Ops:
  7.2 84.7 %all-gather.6.cloned.1.call-start = ((), (), s32[]{:S(2)}) async-start(), calls=%async_computation.4 | async-start | bytes 3981312 | tf_op jit(solution)/shard_map/all_gather | solution.py:188
  7.9 203.1 %all-gather.8.cloned.1.call-start = ((), (), s32[]{:S(2)}) async-start(), calls=%async_computation.5 | async-start | bytes 1327104 | tf_op jit(solution)/shard_map/all_gather | solution.py:190
  8.7 208.4 %all-gather.10.cloned.1.call-start = ((), (), s32[]{:S(2)}) async-start(), calls=%async_computation.6 | async-start | bytes 5308416 | tf_op jit(solution)/shard_map/all_gather | solution.py:194
  9.4 271.1 %all-gather.12.cloned.1.call-start = ((), (), s32[]{:S(2)}) async-start(), calls=%async_computation.7 | async-start | bytes 5308416 | tf_op jit(solution)/shard_map/all_gather | solution.py:254
  10.0 947.6 %reduce-scatter.7.cloned.1.call-start = ((), (), s32[]{:S(2)}) async-start(), calls=%async_computation.9 | async-start | bytes 2654208 | tf_op jit(solution)/shard_map/reduce_scatter | solution.py:328
  61.9 149.1 %copy-start.1 = (bf16[1024,768]{0,1:T(8,128)(2,1)}, bf16[1024,768]{0,1:T(8,128)(2,1)S(1)}, u32[]{:S(2)}) copy-start(bf16[1024,768]{0,1:T(8,128)(2,1)S(1)} %copy.80) | copy-start | bytes 4718596
  62.8 47.1 %copy-start.22 = (f32[12,32]{1,0:T(8,128)}, f32[12,32]{1,0:T(8,128)S(1)}, u32[]{:S(2)}) copy-start(f32[12,32]{1,0:T(8,128)S(1)} %slice.79) | copy-start | bytes 4612
  62.9 47.0 %copy-start.24 = (f32[12,32]{1,0:T(8,128)}, f32[12,32]{1,0:T(8,128)S(1)}, u32[]{:S(2)}) copy-start(f32[12,32]{1,0:T(8,128)S(1)} %slice.81) | copy-start | bytes 4612
  217.1 63.4 %copy-start.19 = (bf16[1024,768]{1,0:T(8,128)(2,1)S(1)}, bf16[1024,768]{1,0:T(8,128)(2,1)}, u32[]{:S(2)}) copy-start(bf16[1024,768]{1,0:T(8,128)(2,1)} %param.35) | copy-start | bytes 4718596
  312.3 646.9 %reduce-scatter.5.cloned.1.call-start = ((), (), s32[]{:S(2)}) async-start(), calls=%async_computation.8 | async-start | bytes 7962624 | tf_op jit(solution)/shard_map/reduce_scatter | solution.py:326
  317.0 233.1 %copy-start.3 = (f32[1024,768]{0,1:T(8,128)S(1)}, f32[1024,768]{0,1:T(8,128)}, u32[]{:S(2)}) copy-start(f32[1024,768]{0,1:T(8,128)} %copy.81) | copy-start | bytes 9437188
  317.0 233.1 %copy-start.23 = (f32[12,32]{1,0:T(8,128)S(1)}, f32[12,32]{1,0:T(8,128)}, u32[]{:S(2)}) copy-start(f32[12,32]{1,0:T(8,128)} %copy-done.22) | copy-start | bytes 4612
  317.0 233.1 %copy-start.25 = (f32[12,32]{1,0:T(8,128)S(1)}, f32[12,32]{1,0:T(8,128)}, u32[]{:S(2)}) copy-start(f32[12,32]{1,0:T(8,128)} %copy-done.24) | copy-start | bytes 4612
  317.0 233.1 %copy-start.29 = (f32[1024]{0:T(1024)S(1)}, f32[1024]{0:T(1024)}, u32[]{:S(2)}) copy-start(f32[1024]{0:T(1024)} %copy-done.28) | copy-start | bytes 12292
  317.1 233.1 %copy-start.31 = (f32[1024]{0:T(1024)S(1)}, f32[1024]{0:T(1024)}, u32[]{:S(2)}) copy-start(f32[1024]{0:T(1024)} %copy-done.30) | copy-start | bytes 12292
  580.9 392.7 %reduce-scatter.9.cloned.1.call-start = ((), (), s32[]{:S(2)}) async-start(), calls=%async_computation.10 | async-start | bytes 10616832 | tf_op jit(solution)/shard_map/reduce_scatter | solution.py:332
  591.7 546.7 %reduce-scatter.11.cloned.1.call-start = ((), (), s32[]{:S(2)}) async-start(), calls=%async_computation.11 | async-start | bytes 10616832 | tf_op jit(solution)/shard_map/reduce_scatter | solution.py:334
  603.3 85.6 %copy-start.38 = (bf16[768]{0:T(1024)(128)(2,1)S(1)}, bf16[768]{0:T(1024)(128)(2,1)}, u32[]{:S(2)}) copy-start(bf16[768]{0:T(1024)(128)(2,1)} %get-tuple-element.431) | copy-start | bytes 4612
  603.3 584.2 %all-reduce.24.cloned.1.call-start = ((), (), s32[]{:S(2)}) async-start(), calls=%async_computation.12 | async-start | bytes 3538944 | tf_op jit(solution)/shard_map/psum | solution.py:341
  604.3 27.5 %collective-permute-start = (bf16[384,768]{1,0:T(8,128)(2,1)S(1)}, bf16[384,768]{1,0:T(8,128)(2,1)S(1)}, u32[]{:S(2)}, u32[]{:S(2)}) collective-permute-start(bf16[384,768]{1,0:T(8,128)(2,1)S(1)} %copy-done.8), channel_id=1, source_target_pairs={{0,28},{4,0},{8,4},{12,8},{16,12},{20,16},{24,20},{28,24},{1,29},{... | collective-permute-start | bytes 1769480 | tf_op jit(solution)/shard_map/ppermute | solution.py:19
  631.8 52.7 %copy-start.12 = (bf16[384,768]{1,0:T(8,128)(2,1)}, bf16[384,768]{1,0:T(8,128)(2,1)S(1)}, u32[]{:S(2)}) copy-start(bf16[384,768]{1,0:T(8,128)(2,1)S(1)} %collective-permute-done) | copy-start | bytes 1769476
  631.9 51.1 %collective-permute-start.1 = (bf16[768,768]{1,0:T(8,128)(2,1)S(1)}, bf16[768,768]{1,0:T(8,128)(2,1)S(1)}, u32[]{:S(2)}, u32[]{:S(2)}) collective-permute-start(bf16[768,768]{1,0:T(8,128)(2,1)S(1)} %pad_maximum_fusion.6), channel_id=1, source_target_pairs={{0,24},{4,28},{8,0},{12,4},{16,8},{20,12},{24,16},{28,20},{1,25},{... | collective-permute-start | bytes 3538952 | tf_op jit(solution)/shard_map/ppermute | solution.py:19
  684.6 183.1 %collective-permute-start.2 = (bf16[1536,768]{1,0:T(8,128)(2,1)}, bf16[1536,768]{1,0:T(8,128)(2,1)}, u32[]{:S(2)}, u32[]{:S(2)}) collective-permute-start(bf16[1536,768]{1,0:T(8,128)(2,1)} %pad_maximum_fusion.1), channel_id=1, source_target_pairs={{0,16},{4,20},{8,24},{12,28},{16,0},{20,4},{24,8},{28,12},{1,17},{... | collective-permute-start | bytes 7077896 | tf_op jit(solution)/shard_map/ppermute | solution.py:19
  692.8 178.9 %copy-start.13 = (bf16[384,768]{1,0:T(8,128)(2,1)S(1)}, bf16[384,768]{1,0:T(8,128)(2,1)}, u32[]{:S(2)}) copy-start(bf16[384,768]{1,0:T(8,128)(2,1)} %copy-done.12) | copy-start | bytes 1769476
  (44 other events, 364.4 us)
Sparse Core Ops, SparseCore 0:
  10.2 67.9 all-gather.5
  80.3 39.9 all-gather.7
  122.5 78.1 all-gather.9
  202.7 77.6 all-gather.11
  312.4 67.9 reduce-scatter.6
  581.0 201.8 reduce-scatter.4
  786.5 187.0 reduce-scatter.8
  977.2 161.2 reduce-scatter.10
  1142.2 45.2 all-reduce.23
